TPU v7x, 512 devices: a whole 4x4x16 slice. The times are simulated.
512 devices in a mesh: col: 4 (over x_lo, core), gx: 16 (over z), gy: 8 (over x_hi, y).
Axes of the slice: x: 4 (x_hi: 2, x_lo: 2; x = x_hi * 2 + x_lo), y: 4, z: 16, core: 2. Of those that a mesh axis runs over, the one named last changes fastest.
Arguments:
- volume: float32 [32, 8, 64, 1024], P('col', None, 'gx', 'gy'), may hold values from -6 to 6
- filters: float32 [32, 32, 3, 3, 3], P('col'), may hold values from -0.21875 to 0.21875
- upstream: float32 [32, 8, 64, 1024], P('col', None, 'gx', 'gy'), may hold values from -6 to 6
Outputs:
- response: float32 [32, 8, 64, 1024], P('col', None, 'gx', 'gy')
- input_grad: float32 [32, 8, 64, 1024], P('col', None, 'gx', 'gy')
- filter_grad: float32 [32, 32, 3, 3, 3], P('col')
All inputs are finite; a program needn't handle non-finite values.
Results may differ from a plain program's by a relative error of at most 0.0003.
Values sent between devices are 32-bit elements; how exact they have to be, the bound alone decides.
No kernel may reach another device: no remote copies, remote signals or barrier semaphores. Data moves between devices by JAX's collectives and lax.ppermute only.
A program may use at most 64 MiB of HBM per device.

v0:
```python
import jax
import jax.numpy as jnp
from jax import lax
from jax.sharding import PartitionSpec as P


def with_halo(block, sides, width):
    for axis, dim in sides:
        count = lax.axis_size(axis)
        forward = [(i, i + 1) for i in range(count - 1)]
        backward = [(target, source) for source, target in forward]
        low = lax.ppermute(
            lax.slice_in_dim(block, block.shape[dim] - width, None, axis=dim), axis, forward
        )
        high = lax.ppermute(lax.slice_in_dim(block, 0, width, axis=dim), axis, backward)
        block = jnp.concatenate([low, block, high], axis=dim)
    return block


def pad_depth(field):
    return jnp.pad(field, ((0, 0), (1, 1), (0, 0), (0, 0)))


def forward_conv(padded, weights, planes, rows_x, rows_y):
    output = jnp.zeros((weights.shape[0], planes, rows_x, rows_y), jnp.float32)
    for depth in range(3):
        for across in range(3):
            for along in range(3):
                window = padded[
                    :, depth : depth + planes, across : across + rows_x, along : along + rows_y
                ]
                output = output + jnp.einsum(
                    "oc,czxy->ozxy",
                    weights[:, :, depth, across, along],
                    window,
                    precision=lax.Precision.HIGHEST,
                )
    return output


def backward_conv(padded_up, weights, planes, rows_x, rows_y):
    output = jnp.zeros((weights.shape[1], planes, rows_x, rows_y), jnp.float32)
    for depth in range(3):
        for across in range(3):
            for along in range(3):
                window = padded_up[
                    :,
                    2 - depth : 2 - depth + planes,
                    2 - across : 2 - across + rows_x,
                    2 - along : 2 - along + rows_y,
                ]
                output = output + jnp.einsum(
                    "oc,ozxy->czxy",
                    weights[:, :, depth, across, along],
                    window,
                    precision=lax.Precision.HIGHEST,
                )
    return output


def weight_terms(cotangent, padded, planes, rows_x, rows_y):
    pieces = []
    for depth in range(3):
        for across in range(3):
            for along in range(3):
                window = padded[
                    :, depth : depth + planes, across : across + rows_x, along : along + rows_y
                ]
                pieces.append(
                    jnp.einsum("ozxy,czxy->oc", cotangent, window, precision=lax.Precision.HIGHEST)
                )
    stacked = jnp.stack(pieces, axis=-1)
    return stacked.reshape(stacked.shape[0], stacked.shape[1], 3, 3, 3)


def shards(volume, filters, upstream):
    planes, rows_x, rows_y = (volume.shape[1], volume.shape[2], volume.shape[3])
    own_inputs = volume.shape[0]
    scale = (planes * rows_x * lax.axis_size("gx") * rows_y * lax.axis_size("gy")) ** (-0.5)
    gathered = lax.all_gather(volume, "col", axis=0, tiled=True)
    padded = pad_depth(with_halo(gathered, (("gx", 2), ("gy", 3)), 1))
    response = forward_conv(padded, filters, planes, rows_x, rows_y)
    all_rows = lax.all_gather(filters, "col", axis=0, tiled=True)
    all_upstream = lax.all_gather(upstream, "col", axis=0, tiled=True)
    padded_up = pad_depth(with_halo(all_upstream, (("gx", 2), ("gy", 3)), 1))
    first = lax.axis_index("col") * own_inputs
    own_filters = lax.dynamic_slice_in_dim(all_rows, first, own_inputs, 1)
    input_grad = backward_conv(padded_up, own_filters, planes, rows_x, rows_y)
    local_grad = weight_terms(upstream, padded, planes, rows_x, rows_y)
    total_grad = lax.psum(local_grad, ("gx", "gy"))
    return (response, input_grad, total_grad * scale)


def solution(mesh):
    placed = (
        P("col", None, "gx", "gy"),
        P("col", None, None, None, None),
        P("col", None, "gx", "gy"),
    )
    return jax.shard_map(
        shards,
        mesh=mesh,
        in_specs=placed,
        out_specs=(
            P("col", None, "gx", "gy"),
            P("col", None, "gx", "gy"),
            P("col", None, None, None, None),
        ),
        check_vma=False,
    )
```

profile of v0, /device:TPU:2, one launch (start us, length us, event | category | flops | bytes accessed | tf_op | source)
XLA Modules:
  0.0 888.0 jit_solution(7384138758110080891)
XLA Ops:
  1.7 11.6 %all_gather.9 = f32[32,8,4,128]{3,0,2,1:T(8,128)S(1)} all-gather(f32[8,8,4,128]{3,0,2,1:T(8,128)S(1)} %copy.65), channel_id=1, replica_groups=mesh['col'=4,'gx'=16,'gy'=8] {'col'}, dimensions={0}, use_global_device_ids=true | all-gather | bytes 655360 | tf_op jit(solution)/shard_map/all_gather | solution.py:80
  17.5 7.3 all_gather.11
  25.5 4.9 collective-permute-start.4
  31.7 6.6 all_gather.10
  41.8 1.9 collective-permute-start.2
  49.1 2.1 copy.74
  51.1 5.1 collective-permute-start.6
  58.8 1.7 fusion.208
  60.5 2.0 fusion.116
  62.6 2.0 fusion.112
  67.8 2.9 pad_maximum_fusion.9
  70.7 2.1 select_maximum_fusion.2
  73.9 2.0 copy.77
  75.9 1.9 select_maximum_fusion
  104.6 4.3 fusion.309
  108.8 1.8 fusion.212
  110.7 1.8 fusion.214
  112.5 1.7 fusion.216
  114.2 1.8 fusion.218
  116.1 1.8 fusion.220
  119.6 1.9 fusion.224
  121.5 1.9 fusion.226
  123.4 1.8 convolution_bitcast_fusion.6
  125.2 1.9 convolution_bitcast_fusion.7
  127.1 1.9 convolution_bitcast_fusion.8
  129.0 1.8 convolution_bitcast_fusion.9
  131.3 1.8 fusion.210
  138.8 1.8 fusion.206
  141.1 1.8 fusion.204
  144.0 1.8 convolution_bitcast_fusion.10
  153.7 715.1 %psum.7 = f32[8,32,3,3,3]{1,0,4,3,2:T(8,128)} all-reduce(f32[8,32,3,3,3]{1,0,4,3,2:T(8,128)} %bitcast.738), channel_id=1, replica_groups=mesh['col'=4,'gx'=16,'gy'=8] {'gx','gy'}, use_global_device_ids=true, to_apply=%region_0.1 | all-reduce | flops 6912 | bytes 55296 | tf_op jit(solution)/shard_map/psum | solution.py:90
  870.6 2.3 fusion.48
  (230 shorter events, 83.1 us)
Async XLA Ops:
  0.6 31.1 %copy-start.65 = (f32[8,32,3,3,3]{1,0,4,3,2:T(8,128)S(1)}, f32[8,32,3,3,3]{1,0,4,3,2:T(8,128)}, u32[]{:S(2)}) copy-start(f32[8,32,3,3,3]{1,0,4,3,2:T(8,128)} %param.4) | copy-start | bytes 82948
  13.2 26.4 %copy-start.3 = (f32[32,8,4,128]{3,0,2,1:T(8,128)}, f32[32,8,4,128]{3,0,2,1:T(8,128)S(1)}, u32[]{:S(2)}) copy-start(f32[32,8,4,128]{3,0,2,1:T(8,128)S(1)} %all_gather.9) | copy-start | bytes 1572868
  13.9 25.5 %collective-permute-start = (f32[32,8,1,128]{3,0,2,1:T(8,128)S(1)}, f32[32,8,1,128]{3,0,2,1:T(8,128)S(1)}, u32[]{:S(2)}, u32[]{:S(2)}) collective-permute-start(f32[32,8,1,128]{3,0,2,1:T(8,128)S(1)} %get-tuple-element.46), channel_id=1, source_target_pairs={{0,8},{8,16},{16,24},{24,32},{32,40},{40,48},{48,56},{56,64},{64,7... | collective-permute-start | bytes 393224 | tf_op jit(solution)/shard_map/ppermute | solution.py:12
  15.2 24.4 %collective-permute-start.1 = (f32[32,8,1,128]{3,0,2,1:T(8,128)}, f32[32,8,1,128]{3,0,2,1:T(8,128)S(1)}, u32[]{:S(2)}, u32[]{:S(2)}) collective-permute-start(f32[32,8,1,128]{3,0,2,1:T(8,128)} %get-tuple-element.45), channel_id=1, source_target_pairs={{8,0},{16,8},{24,16},{32,24},{40,32},{48,40},{56,48},{64,56},{72,6... | collective-permute-start | bytes 393224 | tf_op jit(solution)/shard_map/ppermute | solution.py:15
  25.5 20.4 %collective-permute-start.4 = (f32[32,8,1,128]{3,0,2,1:T(8,128)}, f32[32,8,1,128]{3,0,2,1:T(8,128)}, u32[]{:S(2)}, u32[]{:S(2)}) collective-permute-start(f32[32,8,1,128]{3,0,2,1:T(8,128)} %get-tuple-element.41), channel_id=1, source_target_pairs={{0,8},{8,16},{16,24},{24,32},{32,40},{40,48},{48,56},{56,64},{64,7... | collective-permute-start | bytes 393224 | tf_op jit(solution)/shard_map/ppermute | solution.py:12
  30.4 16.4 %collective-permute-start.5 = (f32[32,8,1,128]{3,0,2,1:T(8,128)}, f32[32,8,1,128]{3,0,2,1:T(8,128)}, u32[]{:S(2)}, u32[]{:S(2)}) collective-permute-start(f32[32,8,1,128]{3,0,2,1:T(8,128)} %get-tuple-element.40), channel_id=1, source_target_pairs={{8,0},{16,8},{24,16},{32,24},{40,32},{48,40},{56,48},{64,56},{72,6... | collective-permute-start | bytes 393224 | tf_op jit(solution)/shard_map/ppermute | solution.py:15
  41.8 22.8 %collective-permute-start.2 = (f32[32,8,6,1]{0,1,3,2:T(8,128)}, f32[32,8,6,1]{0,1,3,2:T(8,128)}, u32[]{:S(2)}, u32[]{:S(2)}) collective-permute-start(f32[32,8,6,1]{0,1,3,2:T(8,128)} %copy.66), channel_id=1, source_target_pairs={{0,1},{1,2},{2,3},{3,4},{4,5},{5,6},{6,7},{8,9},{9,10},{10,11},{11... | collective-permute-start | bytes 18440 | tf_op jit(solution)/shard_map/ppermute | solution.py:12
  44.6 21.1 %collective-permute-start.3 = (f32[32,8,6,1]{0,1,3,2:T(8,128)}, f32[32,8,6,1]{0,1,3,2:T(8,128)}, u32[]{:S(2)}, u32[]{:S(2)}) collective-permute-start(f32[32,8,6,1]{0,1,3,2:T(8,128)} %copy.67), channel_id=1, source_target_pairs={{1,0},{2,1},{3,2},{4,3},{5,4},{6,5},{7,6},{9,8},{10,9},{11,10},{12... | collective-permute-start | bytes 18440 | tf_op jit(solution)/shard_map/ppermute | solution.py:15
  47.8 11.0 %copy-start.20 = (f32[32,8,5,128]{3,0,2,1:T(8,128)S(1)}, f32[32,8,5,128]{3,0,2,1:T(8,128)}, u32[]{:S(2)}) copy-start(f32[32,8,5,128]{3,0,2,1:T(8,128)} %copy-done.19) | copy-start | bytes 1966084
  51.1 21.6 %collective-permute-start.6 = (f32[32,8,6,1]{0,1,3,2:T(8,128)}, f32[32,8,6,1]{0,1,3,2:T(8,128)}, u32[]{:S(2)}, u32[]{:S(2)}) collective-permute-start(f32[32,8,6,1]{0,1,3,2:T(8,128)} %copy.74), channel_id=1, source_target_pairs={{0,1},{1,2},{2,3},{3,4},{4,5},{5,6},{6,7},{8,9},{9,10},{10,11},{11... | collective-permute-start | bytes 18440 | tf_op jit(solution)/shard_map/ppermute | solution.py:12
  57.2 16.7 %collective-permute-start.7 = (f32[32,8,6,1]{0,1,3,2:T(8,128)}, f32[32,8,6,1]{0,1,3,2:T(8,128)}, u32[]{:S(2)}, u32[]{:S(2)}) collective-permute-start(f32[32,8,6,1]{0,1,3,2:T(8,128)} %copy.75), channel_id=1, source_target_pairs={{1,0},{2,1},{3,2},{4,3},{5,4},{6,5},{7,6},{9,8},{10,9},{11,10},{12... | collective-permute-start | bytes 18440 | tf_op jit(solution)/shard_map/ppermute | solution.py:15
  77.7 22.6 %copy-start.1 = (f32[32,10,6,130]{3,0,2,1:T(8,128)}, f32[32,10,6,130]{3,0,2,1:T(8,128)S(1)}, u32[]{:S(2)}) copy-start(f32[32,10,6,130]{3,0,2,1:T(8,128)S(1)} %select_maximum_fusion) | copy-start | bytes 2995204
  83.7 4.7 copy-start.2
  119.6 11.2 %copy-start = (f32[8,8,4,128]{3,2,1,0:T(4,128)S(1)}, f32[8,8,4,128]{3,2,1,0:T(4,128)}, u32[]{:S(2)}) copy-start(f32[8,8,4,128]{3,2,1,0:T(4,128)} %param.5) | copy-start | bytes 393220
  119.6 11.2 %copy-start.33 = (f32[32,8,4,128]{3,0,2,1:T(8,128)S(1)}, f32[32,8,4,128]{3,0,2,1:T(8,128)}, u32[]{:S(2)}) copy-start(f32[32,8,4,128]{3,0,2,1:T(8,128)} %get-tuple-element.26) | copy-start | bytes 1572868
  121.5 9.8 %copy-start.13 = (f32[32,8,4,128]{3,0,2,1:T(8,128)S(1)}, f32[32,8,4,128]{3,0,2,1:T(8,128)}, u32[]{:S(2)}) copy-start(f32[32,8,4,128]{3,0,2,1:T(8,128)} %get-tuple-element.28) | copy-start | bytes 1572868
  123.4 9.7 %copy-start.32 = (f32[32,8,4,128]{3,0,2,1:T(8,128)S(1)}, f32[32,8,4,128]{3,0,2,1:T(8,128)}, u32[]{:S(2)}) copy-start(f32[32,8,4,128]{3,0,2,1:T(8,128)} %get-tuple-element.25) | copy-start | bytes 1572868
  125.2 8.5 copy-start.31
  127.1 7.1 copy-start.30
  129.0 5.8 copy-start.29
  136.4 4.7 copy-start.11
  137.5 6.0 copy-start.4
  138.1 5.9 copy-start.10
  138.8 7.0 copy-start.14
  140.6 5.8 copy-start.8
  141.1 5.8 copy-start.17
  875.5 4.6 copy-start.18
  875.5 4.6 copy-start.36
  875.5 4.6 copy-start.37
  875.5 4.6 copy-start.38
  875.5 4.6 copy-start.39
  875.5 4.6 copy-start.49
  (43 other events, 128.5 us)
where the time goes:
time: 893 us; the launch traced here: 888 us
  blocking collectives  741 us (83%)
  matrix products  92.9 us (10%)
  local copies, waits for them, and re-layouts  25.6 us (3%)
  starting transfers between devices  18.6 us (2%)
    psum x1, blocking collectives, shards(): total_grad = lax.psum(local_grad, ('gx', 'gy'))  715 us
    dot_general x27, matrix products, forward_conv(): jnp.einsum('oc,czxy->ozxy', weights[:, :, depth, across, along], window,...  42.3 us
    dot_general x27, matrix products, backward_conv(): jnp.einsum('oc,ozxy->czxy', weights[:, :, depth, across, along], window,...  35.7 us
  transfers between devices with their start and end apart: 8, of which 0 were waited for; matrix products, arithmetic and copies ran while one was open for 3% of the time, Pallas kernels for 0%

commit v1 on v0

--- a/solution.py
+++ b/solution.py
@@ -74,6 +74,10 @@
 
 
 def shards(volume, filters, upstream):
+
+    def recast_lines(buf):
+        return jnp.sum(lax.all_gather(buf, axis_name=("gx", "gy")), 0)
+
     planes, rows_x, rows_y = (volume.shape[1], volume.shape[2], volume.shape[3])
     own_inputs = volume.shape[0]
     scale = (planes * rows_x * lax.axis_size("gx") * rows_y * lax.axis_size("gy")) ** (-0.5)
@@ -87,7 +91,7 @@
     own_filters = lax.dynamic_slice_in_dim(all_rows, first, own_inputs, 1)
     input_grad = backward_conv(padded_up, own_filters, planes, rows_x, rows_y)
     local_grad = weight_terms(upstream, padded, planes, rows_x, rows_y)
-    total_grad = lax.psum(local_grad, ("gx", "gy"))
+    total_grad = recast_lines(local_grad)
     return (response, input_grad, total_grad * scale)
 
 

time: 893 us -> 432 us (0.48)
  the two profiles are of different devices: /device:TPU:2 before, /device:TPU:8 now
where the time goes in v1:
time: 432 us; the launch traced here: 428 us
  waiting for transfers between devices  263 us (61%)
  matrix products  67.1 us (16%)
  starting transfers between devices  28.1 us (7%)
  local copies, waits for them, and re-layouts  21.8 us (5%)
  blocking collectives  20.4 us (5%)
  between operations  15.4 us (4%)
  other arithmetic  12 us (3%)
    all_gather x1, waiting for transfers between devices, recast_lines(): return jnp.sum(lax.all_gather(buf, axis_name=('gx', 'gy')), 0)  263 us
    dot_general x27, matrix products, backward_conv(): jnp.einsum('oc,ozxy->czxy', weights[:, :, depth, across, along], window,...  35.6 us
    dot_general x27, matrix products, weight_terms(): jnp.einsum('ozxy,czxy->oc', cotangent, window, precision=lax.Precision.HI...  18.3 us
    ppermute x4, starting transfers between devices, with_halo(): lax.ppermute(lax.slice_in_dim(block, block.shape[dim] - width, None, axis...  14.1 us
    ppermute x4, starting transfers between devices, with_halo(): lax.ppermute(lax.slice_in_dim(block, 0, width, axis=dim), axis, backward)  14 us
    dot_general x27, matrix products, forward_conv(): jnp.einsum('oc,czxy->ozxy', weights[:, :, depth, across, along], window,...  13.2 us
  transfers between devices with their start and end apart: 9, of which 1 were waited for; matrix products, arithmetic and copies ran while one was open for 14% of the time, Pallas kernels for 0%

profile of v1, /device:TPU:8, one launch (start us, length us, event | category | flops | bytes accessed | tf_op | source)
XLA Modules:
  0.0 428.1 jit_solution(17874844922462230376)
XLA Ops:
  8.2 7.2 %all_gather.14 = f32[32,8,4,128]{3,0,2,1:T(8,128)S(1)} all-gather(f32[8,8,4,128]{3,0,2,1:T(8,128)S(1)} %copy.73), channel_id=1, replica_groups=mesh['col'=4,'gx'=16,'gy'=8] {'col'}, dimensions={0}, use_global_device_ids=true | all-gather | bytes 655360 | tf_op jit(solution)/shard_map/all_gather | solution.py:88
  16.1 1.3 collective-permute-start.5
  17.4 5.2 %collective-permute-start.4 = (f32[32,8,1,128]{3,0,2,1:T(8,128)}, f32[32,8,1,128]{3,0,2,1:T(8,128)}, u32[]{:S(2)}, u32[]{:S(2)}) collective-permute-start(f32[32,8,1,128]{3,0,2,1:T(8,128)} %get-tuple-element.41), channel_id=1, source_target_pairs={{0,8},{8,16},{16,24},{24,32},{32,40},{40,48},{48,56},{56,64},{64,7... | collective-permute-start | bytes 393224 | tf_op jit(solution)/shard_map/ppermute | solution.py:12
  23.6 6.9 %all_gather.12 = f32[32,8,4,128]{3,0,2,1:T(8,128)S(1)} all-gather(f32[8,8,4,128]{3,0,2,1:T(8,128)S(1)} %copy.65), channel_id=1, replica_groups=mesh['col'=4,'gx'=16,'gy'=8] {'col'}, dimensions={0}, use_global_device_ids=true | all-gather | bytes 655360 | tf_op jit(solution)/shard_map/all_gather | solution.py:84
  30.5 1.3 collective-permute-start.1
  31.8 4.6 %collective-permute-start = (f32[32,8,1,128]{3,0,2,1:T(8,128)S(1)}, f32[32,8,1,128]{3,0,2,1:T(8,128)S(1)}, u32[]{:S(2)}, u32[]{:S(2)}) collective-permute-start(f32[32,8,1,128]{3,0,2,1:T(8,128)S(1)} %get-tuple-element.46), channel_id=1, source_target_pairs={{0,8},{8,16},{16,24},{24,32},{32,40},{40,48},{48,56},{56,64},{64,7... | collective-permute-start | bytes 393224 | tf_op jit(solution)/shard_map/ppermute | solution.py:12
  36.4 6.3 %all_gather.13 = f32[32,32,3,3,3]{1,0,4,3,2:T(8,128)S(1)} all-gather(f32[8,32,3,3,3]{1,0,4,3,2:T(8,128)S(1)} %copy-done.68), channel_id=1, replica_groups=mesh['col'=4,'gx'=16,'gy'=8] {'col'}, dimensions={0}, use_global_device_ids=true | all-gather | bytes 138240 | tf_op jit(solution)/shard_map/all_gather | solution.py:87
  47.2 7.0 %collective-permute-start.3 = (f32[32,8,6,1]{0,1,3,2:T(8,128)}, f32[32,8,6,1]{0,1,3,2:T(8,128)}, u32[]{:S(2)}, u32[]{:S(2)}) collective-permute-start(f32[32,8,6,1]{0,1,3,2:T(8,128)} %copy.67), channel_id=1, source_target_pairs={{1,0},{2,1},{3,2},{4,3},{5,4},{6,5},{7,6},{9,8},{10,9},{11,10},{12... | collective-permute-start | bytes 18440 | tf_op jit(solution)/shard_map/ppermute | solution.py:15
  54.2 1.9 collective-permute-start.2
  56.1 1.7 fusion.208
  61.4 4.5 %collective-permute-start.7 = (f32[32,8,6,1]{0,1,3,2:T(8,128)S(1)}, f32[32,8,6,1]{0,1,3,2:T(8,128)S(1)}, u32[]{:S(2)}, u32[]{:S(2)}) collective-permute-start(f32[32,8,6,1]{0,1,3,2:T(8,128)S(1)} %copy.75), channel_id=1, source_target_pairs={{1,0},{2,1},{3,2},{4,3},{5,4},{6,5},{7,6},{9,8},{10,9},{11,10},{12... | collective-permute-start | bytes 18440 | tf_op jit(solution)/shard_map/ppermute | solution.py:15
  65.9 2.4 collective-permute-start.6
  68.3 2.0 fusion.116
  70.3 2.0 fusion.112
  72.7 1.2 fusion.80
  76.2 1.3 fusion.94
  88.0 1.2 fusion.122
  96.1 1.3 fusion.86
  97.4 2.0 copy.68
  99.4 2.0 copy.69
  101.4 2.4 select_maximum_fusion.2
  103.9 2.3 pad_maximum_fusion.9
  106.1 5.3 %fusion.309 = (f32[32,8,4,128]{3,0,2,1:T(8,128)}, f32[32,8,4,128]{3,0,2,1:T(8,128)}, f32[32,8,4,128]{3,0,2,1:T(8,128)}, f32[32,8,4,128]{3,0,2,1:T(8,128)}, f32[3...) fusion(f32[32,10,6,130]{3,0,2,1:T(8,128)S(1)} %select_maximum_f, ...), kind=kLoop, calls=%fused_computation.415 | loop fusion | bytes 18874368 | tf_op jit(solution)/shard_map/slice | solution.py:29
  111.5 1.7 fusion.76
  113.2 1.7 fusion.75
  114.9 1.7 fusion.74
  130.8 2.1 fusion.83
  133.0 1.5 fusion.114
  134.6 1.8 fusion.48
  136.6 1.4 fusion.49
  151.2 263.2 %all-gather.2.cloned.1.call-done = f32[128,8,32,3,3,3]{2,1,5,4,3,0:T(8,128)} async-done(((f32[1,8,32,3,3,3]{2,1,5,4,3,0:T(8,128)}), f32[128,8,32,3,3,3]{2,1,5,4,3,0:T(8,128)}) %all-gather.2.cloned.1.call-update) | async-done | bytes 3538960 | tf_op jit(solution)/shard_map/all_gather | solution.py:79
  414.4 6.0 %reduce_sum.9 = f32[8,32,3,3,3]{1,0,4,3,2:T(8,128)S(1)} reduce(f32[128,8,32,3,3,3]{2,1,5,4,3,0:T(8,128)} %all-gather.2.cloned.1.call-done, f32[]{:T(128)} %constant.3.clone.1), dimensions={0}, to_apply=%region_0.1 | reduce | flops 877824 | bytes 3566596 | tf_op jit(solution)/shard_map/reduce_sum | solution.py:79
  (241 shorter events, 58.4 us)
Async XLA Ops:
  7.2 29.2 %copy-start.68 = (f32[8,32,3,3,3]{1,0,4,3,2:T(8,128)S(1)}, f32[8,32,3,3,3]{1,0,4,3,2:T(8,128)}, u32[]{:S(2)}) copy-start(f32[8,32,3,3,3]{1,0,4,3,2:T(8,128)} %param.4) | copy-start | bytes 82948
  7.2 407.2 %all-gather.2.cloned.1.call-start = ((), (), s32[]{:S(2)}) async-start(), calls=%async_computation | async-start | bytes 14266368 | tf_op jit(solution)/shard_map/all_gather | solution.py:79
  16.1 42.7 %collective-permute-start.5 = (f32[32,8,1,128]{3,0,2,1:T(8,128)}, f32[32,8,1,128]{3,0,2,1:T(8,128)}, u32[]{:S(2)}, u32[]{:S(2)}) collective-permute-start(f32[32,8,1,128]{3,0,2,1:T(8,128)} %get-tuple-element.40), channel_id=1, source_target_pairs={{8,0},{16,8},{24,16},{32,24},{40,32},{48,40},{56,48},{64,56},{72,6... | collective-permute-start | bytes 393224 | tf_op jit(solution)/shard_map/ppermute | solution.py:15
  17.4 40.5 %collective-permute-start.4 = (f32[32,8,1,128]{3,0,2,1:T(8,128)}, f32[32,8,1,128]{3,0,2,1:T(8,128)}, u32[]{:S(2)}, u32[]{:S(2)}) collective-permute-start(f32[32,8,1,128]{3,0,2,1:T(8,128)} %get-tuple-element.41), channel_id=1, source_target_pairs={{0,8},{8,16},{16,24},{24,32},{32,40},{40,48},{48,56},{56,64},{64,7... | collective-permute-start | bytes 393224 | tf_op jit(solution)/shard_map/ppermute | solution.py:12
  30.5 13.6 %copy-start.6 = (f32[32,8,4,128]{3,0,2,1:T(8,128)}, f32[32,8,4,128]{3,0,2,1:T(8,128)S(1)}, u32[]{:S(2)}) copy-start(f32[32,8,4,128]{3,0,2,1:T(8,128)S(1)} %all_gather.12) | copy-start | bytes 1572868
  30.5 13.6 %collective-permute-start.1 = (f32[32,8,1,128]{3,0,2,1:T(8,128)S(1)}, f32[32,8,1,128]{3,0,2,1:T(8,128)S(1)}, u32[]{:S(2)}, u32[]{:S(2)}) collective-permute-start(f32[32,8,1,128]{3,0,2,1:T(8,128)S(1)} %get-tuple-element.45), channel_id=1, source_target_pairs={{8,0},{16,8},{24,16},{32,24},{40,32},{48,40},{56,48},{64,56},{72,6... | collective-permute-start | bytes 393224 | tf_op jit(solution)/shard_map/ppermute | solution.py:15
  31.8 12.0 %collective-permute-start = (f32[32,8,1,128]{3,0,2,1:T(8,128)S(1)}, f32[32,8,1,128]{3,0,2,1:T(8,128)S(1)}, u32[]{:S(2)}, u32[]{:S(2)}) collective-permute-start(f32[32,8,1,128]{3,0,2,1:T(8,128)S(1)} %get-tuple-element.46), channel_id=1, source_target_pairs={{0,8},{8,16},{16,24},{24,32},{32,40},{40,48},{48,56},{56,64},{64,7... | collective-permute-start | bytes 393224 | tf_op jit(solution)/shard_map/ppermute | solution.py:12
  44.1 17.3 %copy-start.26 = (f32[32,8,5,128]{3,0,2,1:T(8,128)}, f32[32,8,5,128]{3,0,2,1:T(8,128)S(1)}, u32[]{:S(2)}) copy-start(f32[32,8,5,128]{3,0,2,1:T(8,128)S(1)} %get-tuple-element.43) | copy-start | bytes 1966084
  47.2 52.2 %collective-permute-start.3 = (f32[32,8,6,1]{0,1,3,2:T(8,128)}, f32[32,8,6,1]{0,1,3,2:T(8,128)}, u32[]{:S(2)}, u32[]{:S(2)}) collective-permute-start(f32[32,8,6,1]{0,1,3,2:T(8,128)} %copy.67), channel_id=1, source_target_pairs={{1,0},{2,1},{3,2},{4,3},{5,4},{6,5},{7,6},{9,8},{10,9},{11,10},{12... | collective-permute-start | bytes 18440 | tf_op jit(solution)/shard_map/ppermute | solution.py:15
  54.2 43.2 %collective-permute-start.2 = (f32[32,8,6,1]{0,1,3,2:T(8,128)}, f32[32,8,6,1]{0,1,3,2:T(8,128)}, u32[]{:S(2)}, u32[]{:S(2)}) collective-permute-start(f32[32,8,6,1]{0,1,3,2:T(8,128)} %copy.66), channel_id=1, source_target_pairs={{0,1},{1,2},{2,3},{3,4},{4,5},{5,6},{6,7},{8,9},{9,10},{10,11},{11... | collective-permute-start | bytes 18440 | tf_op jit(solution)/shard_map/ppermute | solution.py:12
  61.0 11.7 %copy-start.43 = (f32[32,32,3,3,3]{1,0,4,3,2:T(8,128)S(1)}, f32[32,32,3,3,3]{1,0,4,3,2:T(8,128)}, u32[]{:S(2)}) copy-start(f32[32,32,3,3,3]{1,0,4,3,2:T(8,128)} %copy-done.42) | copy-start | bytes 331780
  61.4 13.8 %collective-permute-start.7 = (f32[32,8,6,1]{0,1,3,2:T(8,128)S(1)}, f32[32,8,6,1]{0,1,3,2:T(8,128)S(1)}, u32[]{:S(2)}, u32[]{:S(2)}) collective-permute-start(f32[32,8,6,1]{0,1,3,2:T(8,128)S(1)} %copy.75), channel_id=1, source_target_pairs={{1,0},{2,1},{3,2},{4,3},{5,4},{6,5},{7,6},{9,8},{10,9},{11,10},{12... | collective-permute-start | bytes 18440 | tf_op jit(solution)/shard_map/ppermute | solution.py:15
  65.9 6.5 %collective-permute-start.6 = (f32[32,8,6,1]{0,1,3,2:T(8,128)}, f32[32,8,6,1]{0,1,3,2:T(8,128)S(1)}, u32[]{:S(2)}, u32[]{:S(2)}) collective-permute-start(f32[32,8,6,1]{0,1,3,2:T(8,128)} %copy.74), channel_id=1, source_target_pairs={{0,1},{1,2},{2,3},{3,4},{4,5},{5,6},{6,7},{8,9},{9,10},{10,11},{11... | collective-permute-start | bytes 18440 | tf_op jit(solution)/shard_map/ppermute | solution.py:12
  75.5 20.6 %copy-start.2 = (f32[32,8,6,1]{3,0,2,1:T(8,128)}, f32[32,8,6,1]{3,0,2,1:T(8,128)S(1)}, u32[]{:S(2)}) copy-start(f32[32,8,6,1]{3,0,2,1:T(8,128)S(1)} %copy.77) | copy-start | bytes 18436
  76.2 18.8 %copy-start.1 = (f32[32,10,6,130]{3,0,2,1:T(8,128)}, f32[32,10,6,130]{3,0,2,1:T(8,128)S(1)}, u32[]{:S(2)}) copy-start(f32[32,10,6,130]{3,0,2,1:T(8,128)S(1)} %select_maximum_fusion) | copy-start | bytes 2995204
  106.1 14.9 %copy-start.13 = (f32[32,8,4,128]{3,0,2,1:T(8,128)}, f32[32,8,4,128]{3,0,2,1:T(8,128)S(1)}, u32[]{:S(2)}) copy-start(f32[32,8,4,128]{3,0,2,1:T(8,128)S(1)} %get-tuple-element.36) | copy-start | bytes 1572868
  106.1 15.5 %copy-start.17 = (f32[32,8,4,128]{3,0,2,1:T(8,128)}, f32[32,8,4,128]{3,0,2,1:T(8,128)S(1)}, u32[]{:S(2)}) copy-start(f32[32,8,4,128]{3,0,2,1:T(8,128)S(1)} %get-tuple-element.29) | copy-start | bytes 1572868
  106.1 17.1 %copy-start.11 = (f32[32,8,4,128]{3,0,2,1:T(8,128)}, f32[32,8,4,128]{3,0,2,1:T(8,128)S(1)}, u32[]{:S(2)}) copy-start(f32[32,8,4,128]{3,0,2,1:T(8,128)S(1)} %get-tuple-element.27) | copy-start | bytes 1572868
  106.1 18.2 %copy-start.15 = (f32[32,8,4,128]{3,0,2,1:T(8,128)}, f32[32,8,4,128]{3,0,2,1:T(8,128)S(1)}, u32[]{:S(2)}) copy-start(f32[32,8,4,128]{3,0,2,1:T(8,128)S(1)} %get-tuple-element.35) | copy-start | bytes 1572868
  106.1 5.4 %copy-start = (f32[8,8,4,128]{3,2,1,0:T(4,128)S(1)}, f32[8,8,4,128]{3,2,1,0:T(4,128)}, u32[]{:S(2)}) copy-start(f32[8,8,4,128]{3,2,1,0:T(4,128)} %param.5) | copy-start | bytes 393220
  111.5 5.1 %copy-start.41 = (f32[32,8,4,128]{3,0,2,1:T(8,128)S(1)}, f32[32,8,4,128]{3,0,2,1:T(8,128)}, u32[]{:S(2)}) copy-start(f32[32,8,4,128]{3,0,2,1:T(8,128)} %get-tuple-element.23) | copy-start | bytes 1572868
  111.5 5.6 %copy-start.40 = (f32[32,8,4,128]{3,0,2,1:T(8,128)S(1)}, f32[32,8,4,128]{3,0,2,1:T(8,128)}, u32[]{:S(2)}) copy-start(f32[32,8,4,128]{3,0,2,1:T(8,128)} %get-tuple-element.22) | copy-start | bytes 1572868
  111.5 6.2 %copy-start.39 = (f32[32,8,4,128]{3,0,2,1:T(8,128)S(1)}, f32[32,8,4,128]{3,0,2,1:T(8,128)}, u32[]{:S(2)}) copy-start(f32[32,8,4,128]{3,0,2,1:T(8,128)} %get-tuple-element.21) | copy-start | bytes 1572868
  113.2 5.6 %copy-start.38 = (f32[32,8,4,128]{3,0,2,1:T(8,128)S(1)}, f32[32,8,4,128]{3,0,2,1:T(8,128)}, u32[]{:S(2)}) copy-start(f32[32,8,4,128]{3,0,2,1:T(8,128)} %get-tuple-element.19) | copy-start | bytes 1572868
  114.9 4.5 %copy-start.37 = (f32[32,8,4,128]{3,0,2,1:T(8,128)S(1)}, f32[32,8,4,128]{3,0,2,1:T(8,128)}, u32[]{:S(2)}) copy-start(f32[32,8,4,128]{3,0,2,1:T(8,128)} %get-tuple-element.18) | copy-start | bytes 1572868
  130.7 3.9 copy-start.45
  130.7 3.9 copy-start.46
  130.7 3.9 copy-start.47
  130.7 3.9 copy-start.58
  130.7 3.9 copy-start.59
  130.7 3.9 copy-start.60
  130.7 3.9 copy-start.61
  (48 other events, 141.3 us)
Sparse Core Ops, SparseCore 0:
  130.8 283.5 all-gather.1
